TPU v7x, 32 devices: a whole 2x2x4 slice. The times are simulated.
32 devices in a mesh: groups: 2 (over y), space: 8 (over z, core), member: 2 (over x).
Axes of the slice: x: 2, y: 2, z: 4, core: 2. Of those that a mesh axis runs over, the one named last changes fastest.
Arguments:
- features: bfloat16 [4, 256, 128, 256], P(('groups', 'member'), None, 'space'), parts along dimension 0, may hold values from -6 to 6
- views: int32 [4], P('groups'), parts along dimension 0, may hold values from 8 to 29
- conv_first: bfloat16 [3, 3, 256, 256], replicated, may hold values from -0.125 to 0.125
- bias_first: float32 [256], replicated, may hold values from -3 to 3
- conv_second: bfloat16 [3, 3, 256, 256], replicated, may hold values from -0.125 to 0.125
- bias_second: float32 [256], replicated, may hold values from -3 to 3
- classify: bfloat16 [19, 256], replicated, may hold values from -0.375 to 0.375
- class_bias: float32 [19], replicated, may hold values from -3 to 3
Outputs:
- ensemble_logits: float32 [1024, 19, 1024], P(('groups', 'space', 'member')), parts along dimension 0
There are 2 independent parts, one for each index of `groups`. A program takes and returns all parts, laid end to end along the dimension named above; an argument that names none is the same for every part. Nothing has to cross between parts.
All inputs are finite; a program needn't handle non-finite values.
Results may differ from a plain program's by a relative error of at most 0.0035.
Values may be sent and summed in bfloat16 or wider, within the bound.
No kernel may reach another device: no remote copies, remote signals or barrier semaphores. Data moves between devices by JAX's collectives and lax.ppermute only.
A program may use at most 128 MiB of HBM per device.

v0:
```python
import jax
import jax.numpy as jnp
from jax import lax
from jax.sharding import PartitionSpec as P

UP = 4


def with_halo(block, sides, width):
    for axis, dim in sides:
        count = lax.axis_size(axis)
        forward = [(i, i + 1) for i in range(count - 1)]
        backward = [(target, source) for source, target in forward]
        low = lax.ppermute(
            lax.slice_in_dim(block, block.shape[dim] - width, None, axis=dim), axis, forward
        )
        high = lax.ppermute(lax.slice_in_dim(block, 0, width, axis=dim), axis, backward)
        block = jnp.concatenate([low, block, high], axis=dim)
    return block


def resize_matrix(positions, out_len, valid, in_len):
    numer = (2 * positions + 1) * valid - out_len
    denom = 2 * out_len
    lower = numer // denom
    frac = (numer - lower * denom).astype(jnp.float32) / denom
    below = numer < 0
    frac = jnp.where(below, jnp.float32(0.0), frac)
    lower = jnp.where(below, 0, lower)
    top_index = valid - 1
    over = lower >= top_index
    frac = jnp.where(over, jnp.float32(0.0), frac)
    lower = jnp.where(over, top_index, lower)
    columns = jnp.arange(in_len, dtype=jnp.int32)
    first = jnp.where(columns[None, :] == lower[:, None], 1.0 - frac[:, None], jnp.float32(0.0))
    second = jnp.where(columns[None, :] == lower[:, None] + 1, frac[:, None], jnp.float32(0.0))
    return (first + second).astype(jnp.bfloat16)


def convolve(field, weights):
    height, width = (field.shape[1], field.shape[2])
    padded = with_halo(field, (("space", 1),), 1)
    padded = jnp.pad(padded, ((0, 0), (0, 0), (1, 1)))
    total = jnp.zeros((weights.shape[2], height, width), jnp.float32)
    for row_tap in range(3):
        for col_tap in range(3):
            window = padded[:, row_tap : row_tap + height, col_tap : col_tap + width]
            total = total + jnp.einsum(
                "oc,cyx->oyx", weights[row_tap, col_tap], window, preferred_element_type=jnp.float32
            )
    return total


def window_start(numer, first_row, full_rows, out_rows, window_rows):
    valid = full_rows * numer // 14
    numer_pos = (2 * first_row + 1) * valid - out_rows
    lower = numer_pos // (2 * out_rows)
    lower = jnp.where(numer_pos < 0, 0, lower)
    lower = jnp.where(lower >= valid - 1, valid - 1, lower)
    return jnp.clip(lower, 0, full_rows - window_rows)


def column_table(numer, flip, cols, out_cols):
    valid_cols = cols * numer // 14
    col_pos = jnp.arange(out_cols, dtype=jnp.int32)
    col_pos = jnp.where(flip == 1, out_cols - 1 - col_pos, col_pos)
    return resize_matrix(col_pos, out_cols, valid_cols, cols)


def shards(features, views, conv_first, bias_first, conv_second, bias_second, classify, class_bias):
    feat = features[0]
    rows_dev, cols = (feat.shape[1], feat.shape[2])
    spaces = lax.axis_size("space")
    full_rows = rows_dev * spaces
    place = lax.axis_index("space")
    member_index = lax.axis_index("member")
    members = views.shape[0]
    picked = jnp.arange(members, dtype=jnp.int32) == member_index
    code = jnp.sum(jnp.where(picked, views, 0))
    numer = code // 2
    valid_rows = full_rows * numer // 14
    valid_cols = cols * numer // 14
    row_ids = place * rows_dev + jnp.arange(rows_dev, dtype=jnp.int32)
    row_ok = row_ids < valid_rows
    col_ok = jnp.arange(cols, dtype=jnp.int32) < valid_cols
    mask = (row_ok[:, None] & col_ok[None, :]).astype(jnp.float32)
    first = feat * mask.astype(jnp.bfloat16)
    hidden = (jax.nn.relu(convolve(first, conv_first) + bias_first[:, None, None]) * mask).astype(
        jnp.bfloat16
    )
    second = (
        jax.nn.relu(convolve(hidden, conv_second) + bias_second[:, None, None]) * mask
    ).astype(jnp.bfloat16)
    logits = (
        jnp.einsum("kc,cyx->kyx", classify, second, preferred_element_type=jnp.float32)
        + class_bias[:, None, None]
    ).astype(jnp.bfloat16)
    out_rows = UP * full_rows
    out_cols = UP * cols
    own_rows = out_rows // spaces
    part_rows = own_rows // members
    window_rows = (part_rows - 1) // UP + 3
    gathered = lax.all_gather(logits, "space", axis=1, tiled=True)
    pieces = []
    for target in range(members):
        first_row = place * own_rows + target * part_rows
        begin = window_start(numer, first_row, full_rows, out_rows, window_rows)
        pieces.append(lax.dynamic_slice_in_dim(gathered, begin, window_rows, 1))
    outgoing = jnp.stack(pieces, 0)
    incoming = lax.all_to_all(outgoing, "member", split_axis=0, concat_axis=0, tiled=True)
    own_first = place * own_rows + member_index * part_rows
    positions = own_first + jnp.arange(part_rows, dtype=jnp.int32)
    result = jnp.zeros((part_rows, logits.shape[0], out_cols), jnp.float32)
    for source in range(members):
        source_numer = views[source] // 2
        source_flip = views[source] % 2
        source_valid = full_rows * source_numer // 14
        begin = window_start(source_numer, own_first, full_rows, out_rows, window_rows)
        source_cols = column_table(source_numer, source_flip, cols, out_cols)
        row_table = resize_matrix(positions, out_rows, source_valid, full_rows)
        row_part = lax.dynamic_slice_in_dim(row_table, begin, window_rows, 1)
        widened = jnp.einsum(
            "cyx,jx->cyj", incoming[source], source_cols, preferred_element_type=jnp.float32
        ).astype(jnp.bfloat16)
        result = result + jnp.einsum(
            "iy,cyj->icj", row_part, widened, preferred_element_type=jnp.float32
        )
    return result


def solution(mesh):
    placed = (
        P(("groups", "member"), None, "space", None),
        P("groups"),
        P(),
        P(),
        P(),
        P(),
        P(),
        P(),
    )
    return jax.shard_map(
        shards,
        mesh=mesh,
        in_specs=placed,
        out_specs=P(("groups", "space", "member"), None, None),
        check_vma=False,
    )
```

profile of v0, /device:TPU:0, one launch (start us, length us, event | category | flops | bytes accessed | tf_op | source)
XLA Modules:
  0.0 144.4 jit_solution(15678336219757409563)
XLA Ops:
  6.5 1.3 fusion.170
  10.5 4.3 %copy.22 = bf16[1,256,16,256]{1,3,2,0:T(8,128)(2,1)} copy(bf16[1,256,16,256]{3,2,1,0:T(8,128)(2,1)} %param.8) | data formatting | bytes 4194304 | tf_op args[0]
  14.9 2.1 %bitcast_multiply_fusion = bf16[256,16,256]{0,2,1:T(8,128)(2,1)S(1)} fusion(bf16[1,256,16,256]{1,3,2,0:T(8,128)(2,1)} %copy.22, bf16[16,256]{1,0:T(8,128)(2,1)S(1)} %get-tuple-element.21), kind=kLoop, calls=%fused_computation.54 | loop fusion | flops 1048576 | bytes 4202496 | tf_op jit(solution)/shard_map/mul | solution.py:87
  17.0 2.5 %collective-permute-start = (bf16[256,1,256]{0,2,1:T(8,128)(2,1)S(1)}, bf16[256,1,256]{0,2,1:T(8,128)(2,1)S(1)}, u32[]{:S(2)}, u32[]{:S(2)}) collective-permute-start(bf16[256,1,256]{0,2,1:T(8,128)(2,1)S(1)} %get-tuple-element.15), channel_id=1, source_target_pairs={{0,2},{2,4},{4,6},{6,8},{8,10},{10,12},{12,14},{1,3},{3,5},{5,7},{... | collective-permute-start | bytes 393224 | tf_op jit(solution)/shard_map/ppermute | solution.py:14
  19.5 1.3 collective-permute-start.1
  20.9 1.7 %fusion.52 = f32[16,256,256]{2,1,0:T(8,128)S(1)} fusion(bf16[256,16,256]{2,1,0:T(8,128)(2,1)S(1)} %multiply_bitcast_fusion, bf16[3,3,256,256]{3,2,1,0:T(8,128)(2,1)S(1)} %copy-done.2), kind=kOutput, calls=%fused_computation.55 | convolution fusion | flops 536870912 | bytes 6422528 | tf_op jit(solution)/shard_map/oc,cyx->oyx/dot_general | solution.py:48
  22.6 2.3 %collective-permute-done.1 = bf16[256,1,256]{0,2,1:T(8,128)(2,1)S(1)} collective-permute-done((bf16[256,1,256]{0,2,1:T(8,128)(2,1)S(1)}, bf16[256,1,256]{0,2,1:T(8,128)(2,1)S(1)}, u32[]{:S(2)}, u32[]{:S(2)}) %collective-permute-start.1) | collective-permute-done | bytes 131104 | tf_op jit(solution)/shard_map/ppermute | solution.py:17
  26.5 2.8 %fusion.42 = f32[16,256,256]{2,1,0:T(8,128)} fusion(bf16[256,18,258]{0,2,1:T(8,128)(2,1)S(1)} %fusion.5, bf16[3,3,256,256]{3,2,1,0:T(8,128)(2,1)S(1)} %copy-done.2), kind=kOutput, calls=%fused_computation.44 | convolution fusion | flops 536870912 | bytes 6422528 | tf_op jit(solution)/shard_map/oc,cyx->oyx/dot_general | solution.py:48
  29.3 2.7 %fusion.44 = f32[16,256,256]{2,1,0:T(8,128)} fusion(bf16[256,18,258]{0,2,1:T(8,128)(2,1)S(1)} %fusion.5, bf16[3,3,256,256]{3,2,1,0:T(8,128)(2,1)S(1)} %copy-done.2), kind=kOutput, calls=%fused_computation.46 | convolution fusion | flops 536870912 | bytes 6422528 | tf_op jit(solution)/shard_map/oc,cyx->oyx/dot_general | solution.py:48
  32.0 2.7 %fusion.46 = f32[16,256,256]{2,1,0:T(8,128)} fusion(bf16[256,18,258]{0,2,1:T(8,128)(2,1)S(1)} %fusion.5, bf16[3,3,256,256]{3,2,1,0:T(8,128)(2,1)S(1)} %copy-done.2), kind=kOutput, calls=%fused_computation.48 | convolution fusion | flops 536870912 | bytes 6422528 | tf_op jit(solution)/shard_map/oc,cyx->oyx/dot_general | solution.py:48
  34.7 2.7 %fusion.48 = f32[16,256,256]{2,1,0:T(8,128)} fusion(bf16[256,18,258]{0,2,1:T(8,128)(2,1)S(1)} %fusion.5, bf16[3,3,256,256]{3,2,1,0:T(8,128)(2,1)S(1)} %copy-done.2), kind=kOutput, calls=%fused_computation.50 | convolution fusion | flops 536870912 | bytes 6422528 | tf_op jit(solution)/shard_map/oc,cyx->oyx/dot_general | solution.py:48
  37.4 2.8 %fusion.6 = f32[16,256,256]{2,1,0:T(8,128)} fusion(bf16[256,16,256]{0,2,1:T(8,128)(2,1)S(1)} %bitcast_multiply_fusion, bf16[256,1,256]{0,2,1:T(8,128)(2,1)S(1)} %collective-permute-done, bf16[3,3,256,256]{3,2,1,0:T(8,128)(2,1)S(1)} %copy-done.2), kind=kOutput, calls=%fused_computation.12 | convolution fusion | flops 541327360 | bytes 6553600 | tf_op jit(solution)/shard_map/oc,cyx->oyx/dot_general | solution.py:48
  40.2 2.7 %fusion.10 = f32[16,256,256]{2,1,0:T(8,128)} fusion(bf16[256,1,256]{0,2,1:T(8,128)(2,1)S(1)} %collective-permute-done.1, bf16[256,16,256]{0,2,1:T(8,128)(2,1)S(1)} %bitcast_multiply_fusion, bf16[3,3,256,256]{3,2,1,0:T(8,128)(2,1)S(1)} %copy-done.2), kind=kOutput, calls=%fused_computation.16 | convolution fusion | flops 541327360 | bytes 6553600 | tf_op jit(solution)/shard_map/oc,cyx->oyx/dot_general | solution.py:48
  42.8 9.7 %fusion.54 = bf16[256,16,256]{0,2,1:T(8,128)(2,1)S(1)} fusion(f32[16,256]{1,0:T(8,128)S(1)} %get-tuple-element.22, f32[256]{0:T(256)S(1)} %copy-done.5, bf16[256,18,258]{0,2,1:T(8,128)(2,1)S(1)} %fusion.5, f32[16,256,256]{2,1,0:T(8,128)} %fusion.10, f32[16,256,256]{2,1,0:T(8,128)S(1)} %fusion.40, f32[16,256,256]{2,1,0:T(8,128)} %fusion.42, ...), kind=kOutput, calls=%fused_computation.59 | convolution fusion | flops 549453824 | bytes 37897216 | tf_op jit(solution)/shard_map/oc,cyx->oyx/dot_general | solution.py:48
  52.6 5.4 %collective-permute-start.2 = (bf16[256,1,256]{0,2,1:T(8,128)(2,1)S(1)}, bf16[256,1,256]{0,2,1:T(8,128)(2,1)S(1)}, u32[]{:S(2)}, u32[]{:S(2)}) collective-permute-start(bf16[256,1,256]{0,2,1:T(8,128)(2,1)S(1)} %get-tuple-element.13), channel_id=1, source_target_pairs={{0,2},{2,4},{4,6},{6,8},{8,10},{10,12},{12,14},{1,3},{3,5},{5,7},{... | collective-permute-start | bytes 393224 | tf_op jit(solution)/shard_map/ppermute | solution.py:14
  58.1 1.5 %collective-permute-start.3 = (bf16[256,1,256]{0,2,1:T(8,128)(2,1)S(1)}, bf16[256,1,256]{0,2,1:T(8,128)(2,1)S(1)}, u32[]{:S(2)}, u32[]{:S(2)}) collective-permute-start(bf16[256,1,256]{0,2,1:T(8,128)(2,1)S(1)} %get-tuple-element.14), channel_id=1, source_target_pairs={{2,0},{4,2},{6,4},{8,6},{10,8},{12,10},{14,12},{3,1},{5,3},{7,5},{... | collective-permute-start | bytes 393224 | tf_op jit(solution)/shard_map/ppermute | solution.py:17
  59.5 3.6 %fusion.108 = f32[16,256,256]{2,1,0:T(8,128)} fusion(bf16[256,16,256]{0,2,1:T(8,128)(2,1)S(1)} %fusion.54, bf16[3,3,256,256]{3,2,1,0:T(8,128)(2,1)} %param.12), kind=kOutput, calls=%fused_computation.91 | convolution fusion | flops 536870912 | bytes 6422528 | tf_op jit(solution)/shard_map/oc,cyx->oyx/dot_general | solution.py:48
  63.1 0.9 select_maximum_fusion
  64.4 2.8 %fusion.26 = f32[16,256,256]{2,1,0:T(8,128)} fusion(bf16[256,18,258]{0,2,1:T(8,128)(2,1)S(1)} %select_maximum_fusion, bf16[3,3,256,256]{3,2,1,0:T(8,128)(2,1)S(1)} %copy-done.3), kind=kOutput, calls=%fused_computation.30 | convolution fusion | flops 536870912 | bytes 6422528 | tf_op jit(solution)/shard_map/oc,cyx->oyx/dot_general | solution.py:48
  67.2 2.7 %fusion.28 = f32[16,256,256]{2,1,0:T(8,128)} fusion(bf16[256,18,258]{0,2,1:T(8,128)(2,1)S(1)} %select_maximum_fusion, bf16[3,3,256,256]{3,2,1,0:T(8,128)(2,1)S(1)} %copy-done.3), kind=kOutput, calls=%fused_computation.32 | convolution fusion | flops 536870912 | bytes 6422528 | tf_op jit(solution)/shard_map/oc,cyx->oyx/dot_general | solution.py:48
  69.9 2.7 %fusion.30 = f32[16,256,256]{2,1,0:T(8,128)} fusion(bf16[256,18,258]{0,2,1:T(8,128)(2,1)S(1)} %select_maximum_fusion, bf16[3,3,256,256]{3,2,1,0:T(8,128)(2,1)S(1)} %copy-done.3), kind=kOutput, calls=%fused_computation.34 | convolution fusion | flops 536870912 | bytes 6422528 | tf_op jit(solution)/shard_map/oc,cyx->oyx/dot_general | solution.py:48
  72.6 2.8 %fusion.32 = f32[16,256,256]{2,1,0:T(8,128)} fusion(bf16[256,18,258]{0,2,1:T(8,128)(2,1)S(1)} %select_maximum_fusion, bf16[3,3,256,256]{3,2,1,0:T(8,128)(2,1)S(1)} %copy-done.3), kind=kOutput, calls=%fused_computation.36 | convolution fusion | flops 536870912 | bytes 6422528 | tf_op jit(solution)/shard_map/oc,cyx->oyx/dot_general | solution.py:48
  75.4 2.7 %fusion.34 = f32[16,256,256]{2,1,0:T(8,128)} fusion(bf16[256,18,258]{0,2,1:T(8,128)(2,1)S(1)} %select_maximum_fusion, bf16[3,3,256,256]{3,2,1,0:T(8,128)(2,1)S(1)} %copy-done.3), kind=kOutput, calls=%fused_computation.38 | convolution fusion | flops 536870912 | bytes 6422528 | tf_op jit(solution)/shard_map/oc,cyx->oyx/dot_general | solution.py:48
  78.1 2.7 %fusion.14 = f32[16,256,256]{2,1,0:T(8,128)} fusion(bf16[256,16,256]{0,2,1:T(8,128)(2,1)S(1)} %fusion.54, bf16[256,1,256]{0,2,1:T(8,128)(2,1)S(1)} %collective-permute-done.2, bf16[3,3,256,256]{3,2,1,0:T(8,128)(2,1)S(1)} %copy-done.3), kind=kOutput, calls=%fused_computation.20 | convolution fusion | flops 541327360 | bytes 6553600 | tf_op jit(solution)/shard_map/oc,cyx->oyx/dot_general | solution.py:48
  80.8 2.7 %fusion.18 = f32[16,256,256]{2,1,0:T(8,128)} fusion(bf16[256,1,256]{0,2,1:T(8,128)(2,1)S(1)} %collective-permute-done.3, bf16[256,16,256]{0,2,1:T(8,128)(2,1)S(1)} %fusion.54, bf16[3,3,256,256]{3,2,1,0:T(8,128)(2,1)S(1)} %copy-done.3), kind=kOutput, calls=%fused_computation.24 | convolution fusion | flops 541327360 | bytes 6553600 | tf_op jit(solution)/shard_map/oc,cyx->oyx/dot_general | solution.py:48
  83.5 13.2 %fusion.72 = bf16[19,16,256]{2,0,1:T(8,128)(2,1)S(1)} fusion(f32[16,256]{1,0:T(8,128)S(1)} %get-tuple-element.22, f32[256]{0:T(256)S(1)} %copy-done.6, bf16[256,18,258]{0,2,1:T(8,128)(2,1)S(1)} %select_maximum_fusion, f32[16,256,256]{2,1,0:T(8,128)} %fusion.18, f32[16,256,256]{2,1,0:T(8,128)} %fusion.26, f32[16,256,256]{2,1,0:T(8,128)} %fusion.28, ...), kind=kOutput, calls=%fused_computation.65 | convolution fusion | flops 589455360 | bytes 35968512 | tf_op jit(solution)/shard_map/kc,cyx->kyx/dot_general | solution.py:95
  103.7 18.8 %all-gather.2.cloned.1.call-done = bf16[19,128,256]{2,1,0:T(8,128)(2,1)} async-done(((bf16[19,16,256]{2,1,0:T(8,128)(2,1)}), bf16[19,128,256]{2,1,0:T(8,128)(2,1)}) %all-gather.2.cloned.1.call-update) | async-done | bytes 1245200 | tf_op jit(solution)/shard_map/all_gather | solution.py:103
  122.6 1.2 constant_dynamic-slice_fusion.1
  124.5 3.4 %all-to-all-start = ((bf16[2,19,10,256]{3,1,2,0:T(8,128)(2,1)}), bf16[2,19,10,256]{3,1,2,0:T(8,128)(2,1)S(1)}, u32[]{:S(2)}, u32[]{:S(2)}) async-start(bf16[2,19,10,256]{3,1,2,0:T(8,128)(2,1)} %pad_maximum_fusion), calls=%async_computation | async-start | bytes 491520 | tf_op jit(solution)/shard_map/all_to_all | solution.py:110
  128.0 5.6 %all-to-all-done = bf16[2,19,10,256]{3,1,2,0:T(8,128)(2,1)S(1)} async-done(((bf16[2,19,10,256]{3,1,2,0:T(8,128)(2,1)}), bf16[2,19,10,256]{3,1,2,0:T(8,128)(2,1)S(1)}, u32[]{:S(2)}, u32[]{:S(2)}) %all-to-all-start) | async-done | bytes 194592 | tf_op jit(solution)/shard_map/all_to_all | solution.py:110
  133.6 1.2 fusion.61
  134.9 2.7 %convolution_add_fusion = f32[32,19,1024]{2,0,1:T(8,128)} fusion(f32[32,19,1024]{2,0,1:T(8,128)S(1)} %fusion.61, f32[1024]{0:T(1024)S(1)} %get-tuple-element.35, s32[1024]{0:T(1024)S(1)} %get-tuple-element.38, f32[1024]{0:T(1024)S(1)} %get-tuple-element.36, s32[1024]{0:T(1024)S(1)} %get-tuple-element.37, ...), kind=kOutput, calls=%fused_computation.58 | convolution fusion | flops 114458816 | bytes 5094916 | tf_op jit(solution)/shard_map/iy,cyj->icj/dot_general | solution.py:125
  (40 shorter events, 4.5 us)
Async XLA Ops:
  6.5 76.9 %copy-start = (bf16[19,256]{1,0:T(8,128)(2,1)S(1)}, bf16[19,256]{1,0:T(8,128)(2,1)}, u32[]{:S(2)}) copy-start(bf16[19,256]{1,0:T(8,128)(2,1)} %param.14) | copy-start | bytes 29188
  6.5 116.0 %all-gather.2.cloned.1.call-start = ((), (), s32[]{:S(2)}) async-start(), calls=%async_computation.1 | async-start | bytes 1400832 | tf_op jit(solution)/shard_map/all_gather | solution.py:103
  14.8 6.0 %copy-start.1 = (bf16[1,256,16,256]{3,2,1,0:T(8,128)(2,1)S(1)}, bf16[1,256,16,256]{3,2,1,0:T(8,128)(2,1)}, u32[]{:S(2)}) copy-start(bf16[1,256,16,256]{3,2,1,0:T(8,128)(2,1)} %param.8) | copy-start | bytes 6291460
  16.9 4.0 %copy-start.2 = (bf16[3,3,256,256]{3,2,1,0:T(8,128)(2,1)S(1)}, bf16[3,3,256,256]{3,2,1,0:T(8,128)(2,1)}, u32[]{:S(2)}) copy-start(bf16[3,3,256,256]{3,2,1,0:T(8,128)(2,1)} %param.10) | copy-start | bytes 3538948
  17.0 5.6 %collective-permute-start = (bf16[256,1,256]{0,2,1:T(8,128)(2,1)S(1)}, bf16[256,1,256]{0,2,1:T(8,128)(2,1)S(1)}, u32[]{:S(2)}, u32[]{:S(2)}) collective-permute-start(bf16[256,1,256]{0,2,1:T(8,128)(2,1)S(1)} %get-tuple-element.15), channel_id=1, source_target_pairs={{0,2},{2,4},{4,6},{6,8},{8,10},{10,12},{12,14},{1,3},{3,5},{5,7},{... | collective-permute-start | bytes 393224 | tf_op jit(solution)/shard_map/ppermute | solution.py:14
  19.5 5.4 %collective-permute-start.1 = (bf16[256,1,256]{0,2,1:T(8,128)(2,1)S(1)}, bf16[256,1,256]{0,2,1:T(8,128)(2,1)S(1)}, u32[]{:S(2)}, u32[]{:S(2)}) collective-permute-start(bf16[256,1,256]{0,2,1:T(8,128)(2,1)S(1)} %get-tuple-element.16), channel_id=1, source_target_pairs={{2,0},{4,2},{6,4},{8,6},{10,8},{12,10},{14,12},{3,1},{5,3},{7,5},{... | collective-permute-start | bytes 393224 | tf_op jit(solution)/shard_map/ppermute | solution.py:17
  40.2 2.7 %copy-start.5 = (f32[256]{0:T(256)S(1)}, f32[256]{0:T(256)}, u32[]{:S(2)}) copy-start(f32[256]{0:T(256)} %param.11) | copy-start | bytes 3076
  52.6 10.5 %collective-permute-start.2 = (bf16[256,1,256]{0,2,1:T(8,128)(2,1)S(1)}, bf16[256,1,256]{0,2,1:T(8,128)(2,1)S(1)}, u32[]{:S(2)}, u32[]{:S(2)}) collective-permute-start(bf16[256,1,256]{0,2,1:T(8,128)(2,1)S(1)} %get-tuple-element.13), channel_id=1, source_target_pairs={{0,2},{2,4},{4,6},{6,8},{8,10},{10,12},{12,14},{1,3},{3,5},{5,7},{... | collective-permute-start | bytes 393224 | tf_op jit(solution)/shard_map/ppermute | solution.py:14
  58.1 5.1 %collective-permute-start.3 = (bf16[256,1,256]{0,2,1:T(8,128)(2,1)S(1)}, bf16[256,1,256]{0,2,1:T(8,128)(2,1)S(1)}, u32[]{:S(2)}, u32[]{:S(2)}) collective-permute-start(bf16[256,1,256]{0,2,1:T(8,128)(2,1)S(1)} %get-tuple-element.14), channel_id=1, source_target_pairs={{2,0},{4,2},{6,4},{8,6},{10,8},{12,10},{14,12},{3,1},{5,3},{7,5},{... | collective-permute-start | bytes 393224 | tf_op jit(solution)/shard_map/ppermute | solution.py:17
  63.1 1.3 copy-start.3
  80.8 2.7 %copy-start.6 = (f32[256]{0:T(256)S(1)}, f32[256]{0:T(256)}, u32[]{:S(2)}) copy-start(f32[256]{0:T(256)} %param.13) | copy-start | bytes 3076
  80.8 2.7 %copy-start.7 = (f32[19]{0:T(128)S(1)}, f32[19]{0:T(128)}, u32[]{:S(2)}) copy-start(f32[19]{0:T(128)} %param.15) | copy-start | bytes 232
  83.5 13.9 %copy-start.4 = (s32[2]{0:T(128)S(1)}, s32[2]{0:T(128)}, u32[]{:S(2)}) copy-start(s32[2]{0:T(128)} %param.9) | copy-start | bytes 28
  124.5 9.1 %all-to-all-start = ((bf16[2,19,10,256]{3,1,2,0:T(8,128)(2,1)}), bf16[2,19,10,256]{3,1,2,0:T(8,128)(2,1)S(1)}, u32[]{:S(2)}, u32[]{:S(2)}) async-start(bf16[2,19,10,256]{3,1,2,0:T(8,128)(2,1)} %pad_maximum_fusion), calls=%async_computation | async-start | bytes 491520 | tf_op jit(solution)/shard_map/all_to_all | solution.py:110
Sparse Core Ops, SparseCore 0:
  97.5 24.9 all-gather.1
where the time goes:
time: 145 us; the launch traced here: 144 us
  matrix products  68.2 us (47%)
  waiting for transfers between devices  26.8 us (18%)
  between operations  21.8 us (15%)
  starting transfers between devices  14.2 us (10%)
  local copies, waits for them, and re-layouts  7.31 us (5%)
  other arithmetic  6.15 us (4%)
    dot_general x17, matrix products, convolve(): jnp.einsum('oc,cyx->oyx', weights[row_tap, col_tap], window, preferred_el...  51.1 us
    all_gather x1, waiting for transfers between devices, shards(): gathered = lax.all_gather(logits, 'space', axis=1, tiled=True)  18.8 us
    dot_general x1, matrix products, shards(): jnp.einsum('kc,cyx->kyx', classify, second, preferred_element_type=jnp.fl...  13.2 us
    ppermute x2, starting transfers between devices, with_halo(): lax.ppermute(lax.slice_in_dim(block, block.shape[dim] - width, None, axis...  7.95 us
    all_to_all x1, waiting for transfers between devices, shards(): lax.all_to_all(outgoing, 'member', split_axis=0, concat_axis=0, tiled=True)  5.63 us
    unnamed x17, local copies, waits for them, and re-layouts  4.69 us
    dot_general x2, matrix products, shards(): jnp.einsum('iy,cyj->icj', row_part, widened, preferred_element_type=jnp.f...  3.89 us
    all_to_all x1, starting transfers between devices, shards(): lax.all_to_all(outgoing, 'member', split_axis=0, concat_axis=0, tiled=True)  3.44 us
  transfers between devices with their start and end apart: 6, of which 3 were waited for; matrix products, arithmetic and copies ran while one was open for 4% of the time, Pallas kernels for 0%

commit v1 on v0

--- a/solution.py
+++ b/solution.py
@@ -4,6 +4,27 @@
 from jax.sharding import PartitionSpec as P
 
 UP = 4
+
+
+def fit_chunk(inp, out_dim):
+    inp = jnp.moveaxis(inp, 0, out_dim)
+    w2 = inp.shape
+    return inp.reshape(*w2[:out_dim], w2[out_dim] * w2[out_dim + 1], *w2[out_dim + 2 :])
+
+
+def hold_limits(obj, link_axis):
+    before, known = (jax.lax.axis_size(link_axis), jax.lax.axis_index(link_axis))
+    earlier, piece_next = (obj[None], 1)
+    while piece_next < before:
+        raw_out = jax.lax.ppermute(
+            earlier, axis_name=link_axis, perm=[(c, c ^ piece_next) for c in range(before)]
+        )
+        g_now = known & piece_next == 0
+        earlier = jnp.concatenate(
+            [jnp.where(g_now, earlier, raw_out), jnp.where(g_now, raw_out, earlier)]
+        )
+        piece_next *= 2
+    return earlier
 
 
 def with_halo(block, sides, width):
@@ -100,7 +121,7 @@
     own_rows = out_rows // spaces
     part_rows = own_rows // members
     window_rows = (part_rows - 1) // UP + 3
-    gathered = lax.all_gather(logits, "space", axis=1, tiled=True)
+    gathered = fit_chunk(hold_limits(logits, "space"), 1)
     pieces = []
     for target in range(members):
         first_row = place * own_rows + target * part_rows

time: 145 us -> 148 us (1.021)
  between operations: 21.8 us -> 8.3 us
  waiting for transfers between devices: 26.8 us -> 39.1 us
  starting transfers between devices: 14.2 us -> 19.7 us
  local copies, waits for them, and re-layouts: 7.31 us -> 5.49 us
    ppermute x0 -> x3, waiting for transfers between devices: none -> 31.8 us  [hold_limits(): jax.lax.ppermute(earlier, axis_name=link_axis, perm=[(c, c ^ piece_next)...]
    all_gather x1 -> x0, waiting for transfers between devices: 18.8 us -> none  [shards(): gathered = lax.all_gather(logits, 'space', axis=1, tiled=True)]
    ppermute x0 -> x3, starting transfers between devices: none -> 5.57 us  [hold_limits(): jax.lax.ppermute(earlier, axis_name=link_axis, perm=[(c, c ^ piece_next)...]
  transfers between devices with their start and end apart: 6 -> 8, of which waited for: 3 -> 5; matrix products, arithmetic and copies ran while one was open for 4% -> 4% of each run, Pallas kernels for 0% -> 0%
where the time goes in v1:
time: 148 us
  matrix products  68.3 us (46%)
  waiting for transfers between devices  39.1 us (26%)
  starting transfers between devices  19.7 us (13%)
  between operations  8.3 us (6%)
  other arithmetic  6.83 us (5%)
  local copies, waits for them, and re-layouts  5.49 us (4%)
    dot_general x17, matrix products, convolve(): jnp.einsum('oc,cyx->oyx', weights[row_tap, col_tap], window, preferred_el...  51.2 us
    ppermute x3, waiting for transfers between devices, hold_limits(): jax.lax.ppermute(earlier, axis_name=link_axis, perm=[(c, c ^ piece_next)...  31.8 us
    dot_general x1, matrix products, shards(): jnp.einsum('kc,cyx->kyx', classify, second, preferred_element_type=jnp.fl...  13.2 us
    ppermute x2, starting transfers between devices, with_halo(): lax.ppermute(lax.slice_in_dim(block, block.shape[dim] - width, None, axis...  7.94 us
    ppermute x3, starting transfers between devices, hold_limits(): jax.lax.ppermute(earlier, axis_name=link_axis, perm=[(c, c ^ piece_next)...  5.57 us
    all_to_all x1, waiting for transfers between devices, shards(): lax.all_to_all(outgoing, 'member', split_axis=0, concat_axis=0, tiled=True)  5.05 us
    unnamed x17, local copies, waits for them, and re-layouts  4.7 us
    dot_general x2, matrix products, shards(): jnp.einsum('iy,cyj->icj', row_part, widened, preferred_element_type=jnp.f...  3.89 us
  transfers between devices with their start and end apart: 8, of which 5 were waited for; matrix products, arithmetic and copies ran while one was open for 4% of the time, Pallas kernels for 0%

profile of v1, /device:TPU:0, one launch (start us, length us, event | category | flops | bytes accessed | tf_op | source)
XLA Modules:
  0.0 147.8 jit_solution(1769030677341943971)
XLA Ops:
  0.0 1.3 fusion.174
  4.0 4.3 %copy.12 = bf16[1,256,16,256]{1,3,2,0:T(8,128)(2,1)} copy(bf16[1,256,16,256]{3,2,1,0:T(8,128)(2,1)} %param.8) | data formatting | bytes 4194304 | tf_op args[0]
  8.3 2.1 %bitcast_multiply_fusion = bf16[256,16,256]{0,2,1:T(8,128)(2,1)S(1)} fusion(bf16[1,256,16,256]{1,3,2,0:T(8,128)(2,1)} %copy.12, bf16[16,256]{1,0:T(8,128)(2,1)S(1)} %get-tuple-element.27), kind=kLoop, calls=%fused_computation.54 | loop fusion | flops 1048576 | bytes 4202496 | tf_op jit(solution)/shard_map/mul | solution.py:108
  10.4 2.5 %collective-permute-start = (bf16[256,1,256]{0,2,1:T(8,128)(2,1)S(1)}, bf16[256,1,256]{0,2,1:T(8,128)(2,1)S(1)}, u32[]{:S(2)}, u32[]{:S(2)}) collective-permute-start(bf16[256,1,256]{0,2,1:T(8,128)(2,1)S(1)} %get-tuple-element.15), channel_id=1, source_target_pairs={{0,2},{2,4},{4,6},{6,8},{8,10},{10,12},{12,14},{1,3},{3,5},{5,7},{... | collective-permute-start | bytes 393224 | tf_op jit(solution)/shard_map/ppermute | solution.py:35
  12.9 1.3 collective-permute-start.1
  14.4 1.7 %fusion.52 = f32[16,256,256]{2,1,0:T(8,128)S(1)} fusion(bf16[256,16,256]{2,1,0:T(8,128)(2,1)S(1)} %multiply_bitcast_fusion, bf16[3,3,256,256]{3,2,1,0:T(8,128)(2,1)S(1)} %copy-done.2), kind=kOutput, calls=%fused_computation.55 | convolution fusion | flops 536870912 | bytes 6422528 | tf_op jit(solution)/shard_map/oc,cyx->oyx/dot_general | solution.py:69
  16.1 2.3 %collective-permute-done.1 = bf16[256,1,256]{0,2,1:T(8,128)(2,1)S(1)} collective-permute-done((bf16[256,1,256]{0,2,1:T(8,128)(2,1)S(1)}, bf16[256,1,256]{0,2,1:T(8,128)(2,1)S(1)}, u32[]{:S(2)}, u32[]{:S(2)}) %collective-permute-start.1) | collective-permute-done | bytes 131104 | tf_op jit(solution)/shard_map/ppermute | solution.py:38
  20.0 2.8 %fusion.42 = f32[16,256,256]{2,1,0:T(8,128)} fusion(bf16[256,18,258]{0,2,1:T(8,128)(2,1)S(1)} %fusion.5, bf16[3,3,256,256]{3,2,1,0:T(8,128)(2,1)S(1)} %copy-done.2), kind=kOutput, calls=%fused_computation.44 | convolution fusion | flops 536870912 | bytes 6422528 | tf_op jit(solution)/shard_map/oc,cyx->oyx/dot_general | solution.py:69
  22.7 2.7 %fusion.44 = f32[16,256,256]{2,1,0:T(8,128)} fusion(bf16[256,18,258]{0,2,1:T(8,128)(2,1)S(1)} %fusion.5, bf16[3,3,256,256]{3,2,1,0:T(8,128)(2,1)S(1)} %copy-done.2), kind=kOutput, calls=%fused_computation.46 | convolution fusion | flops 536870912 | bytes 6422528 | tf_op jit(solution)/shard_map/oc,cyx->oyx/dot_general | solution.py:69
  25.5 2.7 %fusion.46 = f32[16,256,256]{2,1,0:T(8,128)} fusion(bf16[256,18,258]{0,2,1:T(8,128)(2,1)S(1)} %fusion.5, bf16[3,3,256,256]{3,2,1,0:T(8,128)(2,1)S(1)} %copy-done.2), kind=kOutput, calls=%fused_computation.48 | convolution fusion | flops 536870912 | bytes 6422528 | tf_op jit(solution)/shard_map/oc,cyx->oyx/dot_general | solution.py:69
  28.2 2.7 %fusion.48 = f32[16,256,256]{2,1,0:T(8,128)} fusion(bf16[256,18,258]{0,2,1:T(8,128)(2,1)S(1)} %fusion.5, bf16[3,3,256,256]{3,2,1,0:T(8,128)(2,1)S(1)} %copy-done.2), kind=kOutput, calls=%fused_computation.50 | convolution fusion | flops 536870912 | bytes 6422528 | tf_op jit(solution)/shard_map/oc,cyx->oyx/dot_general | solution.py:69
  30.9 2.8 %fusion.6 = f32[16,256,256]{2,1,0:T(8,128)} fusion(bf16[256,16,256]{0,2,1:T(8,128)(2,1)S(1)} %bitcast_multiply_fusion, bf16[256,1,256]{0,2,1:T(8,128)(2,1)S(1)} %collective-permute-done, bf16[3,3,256,256]{3,2,1,0:T(8,128)(2,1)S(1)} %copy-done.2), kind=kOutput, calls=%fused_computation.12 | convolution fusion | flops 541327360 | bytes 6553600 | tf_op jit(solution)/shard_map/oc,cyx->oyx/dot_general | solution.py:69
  33.6 2.7 %fusion.10 = f32[16,256,256]{2,1,0:T(8,128)} fusion(bf16[256,1,256]{0,2,1:T(8,128)(2,1)S(1)} %collective-permute-done.1, bf16[256,16,256]{0,2,1:T(8,128)(2,1)S(1)} %bitcast_multiply_fusion, bf16[3,3,256,256]{3,2,1,0:T(8,128)(2,1)S(1)} %copy-done.2), kind=kOutput, calls=%fused_computation.16 | convolution fusion | flops 541327360 | bytes 6553600 | tf_op jit(solution)/shard_map/oc,cyx->oyx/dot_general | solution.py:69
  36.3 9.7 %fusion.54 = bf16[256,16,256]{0,2,1:T(8,128)(2,1)S(1)} fusion(f32[16,256]{1,0:T(8,128)S(1)} %get-tuple-element.28, f32[256]{0:T(256)S(1)} %copy-done.5, bf16[256,18,258]{0,2,1:T(8,128)(2,1)S(1)} %fusion.5, f32[16,256,256]{2,1,0:T(8,128)} %fusion.10, f32[16,256,256]{2,1,0:T(8,128)S(1)} %fusion.40, f32[16,256,256]{2,1,0:T(8,128)} %fusion.42, ...), kind=kOutput, calls=%fused_computation.59 | convolution fusion | flops 549453824 | bytes 37897216 | tf_op jit(solution)/shard_map/oc,cyx->oyx/dot_general | solution.py:69
  46.1 5.4 %collective-permute-start.2 = (bf16[256,1,256]{0,2,1:T(8,128)(2,1)S(1)}, bf16[256,1,256]{0,2,1:T(8,128)(2,1)S(1)}, u32[]{:S(2)}, u32[]{:S(2)}) collective-permute-start(bf16[256,1,256]{0,2,1:T(8,128)(2,1)S(1)} %get-tuple-element.13), channel_id=1, source_target_pairs={{0,2},{2,4},{4,6},{6,8},{8,10},{10,12},{12,14},{1,3},{3,5},{5,7},{... | collective-permute-start | bytes 393224 | tf_op jit(solution)/shard_map/ppermute | solution.py:35
  51.5 1.5 collective-permute-start.3
  53.0 3.6 %fusion.112 = f32[16,256,256]{2,1,0:T(8,128)} fusion(bf16[256,16,256]{0,2,1:T(8,128)(2,1)S(1)} %fusion.54, bf16[3,3,256,256]{3,2,1,0:T(8,128)(2,1)} %param.12), kind=kOutput, calls=%fused_computation.100 | convolution fusion | flops 536870912 | bytes 6422528 | tf_op jit(solution)/shard_map/oc,cyx->oyx/dot_general | solution.py:69
  57.9 2.8 %fusion.26 = f32[16,256,256]{2,1,0:T(8,128)} fusion(bf16[256,18,258]{0,2,1:T(8,128)(2,1)S(1)} %select_maximum_fusion, bf16[3,3,256,256]{3,2,1,0:T(8,128)(2,1)S(1)} %copy-done.3), kind=kOutput, calls=%fused_computation.30 | convolution fusion | flops 536870912 | bytes 6422528 | tf_op jit(solution)/shard_map/oc,cyx->oyx/dot_general | solution.py:69
  60.7 2.7 %fusion.28 = f32[16,256,256]{2,1,0:T(8,128)} fusion(bf16[256,18,258]{0,2,1:T(8,128)(2,1)S(1)} %select_maximum_fusion, bf16[3,3,256,256]{3,2,1,0:T(8,128)(2,1)S(1)} %copy-done.3), kind=kOutput, calls=%fused_computation.32 | convolution fusion | flops 536870912 | bytes 6422528 | tf_op jit(solution)/shard_map/oc,cyx->oyx/dot_general | solution.py:69
  63.4 2.7 %fusion.30 = f32[16,256,256]{2,1,0:T(8,128)} fusion(bf16[256,18,258]{0,2,1:T(8,128)(2,1)S(1)} %select_maximum_fusion, bf16[3,3,256,256]{3,2,1,0:T(8,128)(2,1)S(1)} %copy-done.3), kind=kOutput, calls=%fused_computation.34 | convolution fusion | flops 536870912 | bytes 6422528 | tf_op jit(solution)/shard_map/oc,cyx->oyx/dot_general | solution.py:69
  66.1 2.8 %fusion.32 = f32[16,256,256]{2,1,0:T(8,128)} fusion(bf16[256,18,258]{0,2,1:T(8,128)(2,1)S(1)} %select_maximum_fusion, bf16[3,3,256,256]{3,2,1,0:T(8,128)(2,1)S(1)} %copy-done.3), kind=kOutput, calls=%fused_computation.36 | convolution fusion | flops 536870912 | bytes 6422528 | tf_op jit(solution)/shard_map/oc,cyx->oyx/dot_general | solution.py:69
  68.9 2.7 %fusion.34 = f32[16,256,256]{2,1,0:T(8,128)} fusion(bf16[256,18,258]{0,2,1:T(8,128)(2,1)S(1)} %select_maximum_fusion, bf16[3,3,256,256]{3,2,1,0:T(8,128)(2,1)S(1)} %copy-done.3), kind=kOutput, calls=%fused_computation.38 | convolution fusion | flops 536870912 | bytes 6422528 | tf_op jit(solution)/shard_map/oc,cyx->oyx/dot_general | solution.py:69
  71.6 2.7 %fusion.14 = f32[16,256,256]{2,1,0:T(8,128)} fusion(bf16[256,16,256]{0,2,1:T(8,128)(2,1)S(1)} %fusion.54, bf16[256,1,256]{0,2,1:T(8,128)(2,1)S(1)} %collective-permute-done.2, bf16[3,3,256,256]{3,2,1,0:T(8,128)(2,1)S(1)} %copy-done.3), kind=kOutput, calls=%fused_computation.20 | convolution fusion | flops 541327360 | bytes 6553600 | tf_op jit(solution)/shard_map/oc,cyx->oyx/dot_general | solution.py:69
  74.4 2.7 %fusion.18 = f32[16,256,256]{2,1,0:T(8,128)} fusion(bf16[256,1,256]{0,2,1:T(8,128)(2,1)S(1)} %collective-permute-done.3, bf16[256,16,256]{0,2,1:T(8,128)(2,1)S(1)} %fusion.54, bf16[3,3,256,256]{3,2,1,0:T(8,128)(2,1)S(1)} %copy-done.3), kind=kOutput, calls=%fused_computation.24 | convolution fusion | flops 541327360 | bytes 6553600 | tf_op jit(solution)/shard_map/oc,cyx->oyx/dot_general | solution.py:69
  77.1 13.2 %fusion.72 = bf16[1,19,16,256]{3,1,2,0:T(8,128)(2,1)S(1)} fusion(f32[16,256]{1,0:T(8,128)S(1)} %get-tuple-element.28, f32[256]{0:T(256)S(1)} %copy-done.6, bf16[256,18,258]{0,2,1:T(8,128)(2,1)S(1)} %select_maximum_fusion, f32[16,256,256]{2,1,0:T(8,128)} %fusion.18, f32[16,256,256]{2,1,0:T(8,128)} %fusion.26, f32[16,256,256]{2,1,0:T(8,128)} %fusion.28, ...), kind=kOutput, calls=%fused_computation.66 | convolution fusion | flops 589455360 | bytes 35968512 | tf_op jit(solution)/shard_map/kc,cyx->kyx/dot_general | solution.py:116
  92.6 1.7 %collective-permute-start.5 = (bf16[2,19,16,256]{3,1,2,0:T(8,128)(2,1)S(1)}, bf16[2,19,16,256]{3,1,2,0:T(8,128)(2,1)S(1)}, u32[]{:S(2)}, u32[]{:S(2)}) collective-permute-start(bf16[2,19,16,256]{3,1,2,0:T(8,128)(2,1)S(1)} %pad_maximum_fusion.2), channel_id=1, source_target_pairs={{0,4},{2,6},{4,0},{6,2},{8,12},{10,14},{12,8},{14,10},{1,5},{3,7},... | collective-permute-start | bytes 933896 | tf_op jit(solution)/shard_map/ppermute | solution.py:19
  94.2 9.8 %collective-permute-done.5 = bf16[2,19,16,256]{3,1,2,0:T(8,128)(2,1)S(1)} collective-permute-done((bf16[2,19,16,256]{3,1,2,0:T(8,128)(2,1)S(1)}, bf16[2,19,16,256]{3,1,2,0:T(8,128)(2,1)S(1)}, u32[]{:S(2)}, u32[]{:S(2)}) %collective-permute-start.5) | collective-permute-done | bytes 311328 | tf_op jit(solution)/shard_map/ppermute | solution.py:19
  104.3 2.7 %collective-permute-start.6 = (bf16[4,19,16,256]{3,2,1,0:T(8,128)(2,1)S(1)}, bf16[4,19,16,256]{3,2,1,0:T(8,128)(2,1)S(1)}, u32[]{:S(2)}, u32[]{:S(2)}) collective-permute-start(bf16[4,19,16,256]{3,2,1,0:T(8,128)(2,1)S(1)} %copy.15), channel_id=1, source_target_pairs={{0,8},{2,10},{4,12},{6,14},{8,0},{10,2},{12,4},{14,6},{1,9},{3,11}... | collective-permute-start | bytes 1867784 | tf_op jit(solution)/shard_map/ppermute | solution.py:19
  113.1 21.0 %collective-permute-done.6 = bf16[4,19,16,256]{3,2,1,0:T(8,128)(2,1)S(1)} collective-permute-done((bf16[4,19,16,256]{3,2,1,0:T(8,128)(2,1)S(1)}, bf16[4,19,16,256]{3,2,1,0:T(8,128)(2,1)S(1)}, u32[]{:S(2)}, u32[]{:S(2)}) %collective-permute-start.6) | collective-permute-done | bytes 622624 | tf_op jit(solution)/shard_map/ppermute | solution.py:19
  135.3 3.4 %all-to-all-start = ((bf16[2,19,10,256]{3,1,2,0:T(8,128)(2,1)}), bf16[2,19,10,256]{3,1,2,0:T(8,128)(2,1)S(1)}, u32[]{:S(2)}, u32[]{:S(2)}) async-start(bf16[2,19,10,256]{3,1,2,0:T(8,128)(2,1)} %pad_maximum_fusion.3), calls=%async_computation | async-start | bytes 491520 | tf_op jit(solution)/shard_map/all_to_all | solution.py:131
  138.8 5.0 %all-to-all-done = bf16[2,19,10,256]{3,1,2,0:T(8,128)(2,1)S(1)} async-done(((bf16[2,19,10,256]{3,1,2,0:T(8,128)(2,1)}), bf16[2,19,10,256]{3,1,2,0:T(8,128)(2,1)S(1)}, u32[]{:S(2)}, u32[]{:S(2)}) %all-to-all-start) | async-done | bytes 194592 | tf_op jit(solution)/shard_map/all_to_all | solution.py:131
  145.1 2.7 %convolution_add_fusion = f32[32,19,1024]{2,0,1:T(8,128)} fusion(f32[32,19,1024]{2,0,1:T(8,128)S(1)} %fusion.61, f32[1024]{0:T(1024)S(1)} %get-tuple-element.39, s32[1024]{0:T(1024)S(1)} %get-tuple-element.42, f32[1024]{0:T(1024)S(1)} %get-tuple-element.40, s32[1024]{0:T(1024)S(1)} %get-tuple-element.41, bf16[19,10,256]{2,0,1:T(8,128)(2,1)S(1)} %get-tuple-element.25, ...), kind=kOutput, calls=%fused_computation.58 | convolution fusion | flops 114458816 | bytes 5094916 | tf_op jit(solution)/shard_map/iy,cyj->icj/dot_general | solution.py:146
  (48 shorter events, 8.9 us)
Async XLA Ops:
  0.0 77.1 %copy-start = (bf16[19,256]{1,0:T(8,128)(2,1)S(1)}, bf16[19,256]{1,0:T(8,128)(2,1)}, u32[]{:S(2)}) copy-start(bf16[19,256]{1,0:T(8,128)(2,1)} %param.14) | copy-start | bytes 29188
  8.2 6.0 %copy-start.1 = (bf16[1,256,16,256]{3,2,1,0:T(8,128)(2,1)S(1)}, bf16[1,256,16,256]{3,2,1,0:T(8,128)(2,1)}, u32[]{:S(2)}) copy-start(bf16[1,256,16,256]{3,2,1,0:T(8,128)(2,1)} %param.8) | copy-start | bytes 6291460
  10.4 4.0 %copy-start.2 = (bf16[3,3,256,256]{3,2,1,0:T(8,128)(2,1)S(1)}, bf16[3,3,256,256]{3,2,1,0:T(8,128)(2,1)}, u32[]{:S(2)}) copy-start(bf16[3,3,256,256]{3,2,1,0:T(8,128)(2,1)} %param.10) | copy-start | bytes 3538948
  10.4 5.6 %collective-permute-start = (bf16[256,1,256]{0,2,1:T(8,128)(2,1)S(1)}, bf16[256,1,256]{0,2,1:T(8,128)(2,1)S(1)}, u32[]{:S(2)}, u32[]{:S(2)}) collective-permute-start(bf16[256,1,256]{0,2,1:T(8,128)(2,1)S(1)} %get-tuple-element.15), channel_id=1, source_target_pairs={{0,2},{2,4},{4,6},{6,8},{8,10},{10,12},{12,14},{1,3},{3,5},{5,7},{... | collective-permute-start | bytes 393224 | tf_op jit(solution)/shard_map/ppermute | solution.py:35
  12.9 5.4 %collective-permute-start.1 = (bf16[256,1,256]{0,2,1:T(8,128)(2,1)S(1)}, bf16[256,1,256]{0,2,1:T(8,128)(2,1)S(1)}, u32[]{:S(2)}, u32[]{:S(2)}) collective-permute-start(bf16[256,1,256]{0,2,1:T(8,128)(2,1)S(1)} %get-tuple-element.16), channel_id=1, source_target_pairs={{2,0},{4,2},{6,4},{8,6},{10,8},{12,10},{14,12},{3,1},{5,3},{7,5},{... | collective-permute-start | bytes 393224 | tf_op jit(solution)/shard_map/ppermute | solution.py:38
  33.6 2.7 %copy-start.5 = (f32[256]{0:T(256)S(1)}, f32[256]{0:T(256)}, u32[]{:S(2)}) copy-start(f32[256]{0:T(256)} %param.11) | copy-start | bytes 3076
  46.1 10.5 %collective-permute-start.2 = (bf16[256,1,256]{0,2,1:T(8,128)(2,1)S(1)}, bf16[256,1,256]{0,2,1:T(8,128)(2,1)S(1)}, u32[]{:S(2)}, u32[]{:S(2)}) collective-permute-start(bf16[256,1,256]{0,2,1:T(8,128)(2,1)S(1)} %get-tuple-element.13), channel_id=1, source_target_pairs={{0,2},{2,4},{4,6},{6,8},{8,10},{10,12},{12,14},{1,3},{3,5},{5,7},{... | collective-permute-start | bytes 393224 | tf_op jit(solution)/shard_map/ppermute | solution.py:35
  51.5 5.1 %collective-permute-start.3 = (bf16[256,1,256]{0,2,1:T(8,128)(2,1)S(1)}, bf16[256,1,256]{0,2,1:T(8,128)(2,1)S(1)}, u32[]{:S(2)}, u32[]{:S(2)}) collective-permute-start(bf16[256,1,256]{0,2,1:T(8,128)(2,1)S(1)} %get-tuple-element.14), channel_id=1, source_target_pairs={{2,0},{4,2},{6,4},{8,6},{10,8},{12,10},{14,12},{3,1},{5,3},{7,5},{... | collective-permute-start | bytes 393224 | tf_op jit(solution)/shard_map/ppermute | solution.py:38
  56.6 1.3 copy-start.3
  74.3 2.7 %copy-start.6 = (f32[256]{0:T(256)S(1)}, f32[256]{0:T(256)}, u32[]{:S(2)}) copy-start(f32[256]{0:T(256)} %param.13) | copy-start | bytes 3076
  74.3 2.7 %copy-start.7 = (f32[19]{0:T(128)S(1)}, f32[19]{0:T(128)}, u32[]{:S(2)}) copy-start(f32[19]{0:T(128)} %param.15) | copy-start | bytes 232
  90.2 2.2 %collective-permute-start.4 = (bf16[1,19,16,256]{3,1,2,0:T(8,128)(2,1)S(1)}, bf16[1,19,16,256]{3,1,2,0:T(8,128)(2,1)S(1)}, u32[]{:S(2)}, u32[]{:S(2)}) collective-permute-start(bf16[1,19,16,256]{3,1,2,0:T(8,128)(2,1)S(1)} %fusion.72), channel_id=1, source_target_pairs={{0,2},{2,0},{4,6},{6,4},{8,10},{10,8},{12,14},{14,12},{1,3},{3,1},... | collective-permute-start | bytes 466952 | tf_op jit(solution)/shard_map/ppermute | solution.py:19
  92.5 14.5 %copy-start.4 = (s32[2]{0:T(128)S(1)}, s32[2]{0:T(128)}, u32[]{:S(2)}) copy-start(s32[2]{0:T(128)} %param.9) | copy-start | bytes 28
  92.6 11.5 %collective-permute-start.5 = (bf16[2,19,16,256]{3,1,2,0:T(8,128)(2,1)S(1)}, bf16[2,19,16,256]{3,1,2,0:T(8,128)(2,1)S(1)}, u32[]{:S(2)}, u32[]{:S(2)}) collective-permute-start(bf16[2,19,16,256]{3,1,2,0:T(8,128)(2,1)S(1)} %pad_maximum_fusion.2), channel_id=1, source_target_pairs={{0,4},{2,6},{4,0},{6,2},{8,12},{10,14},{12,8},{14,10},{1,5},{3,7},... | collective-permute-start | bytes 933896 | tf_op jit(solution)/shard_map/ppermute | solution.py:19
  104.3 29.8 %collective-permute-start.6 = (bf16[4,19,16,256]{3,2,1,0:T(8,128)(2,1)S(1)}, bf16[4,19,16,256]{3,2,1,0:T(8,128)(2,1)S(1)}, u32[]{:S(2)}, u32[]{:S(2)}) collective-permute-start(bf16[4,19,16,256]{3,2,1,0:T(8,128)(2,1)S(1)} %copy.15), channel_id=1, source_target_pairs={{0,8},{2,10},{4,12},{6,14},{8,0},{10,2},{12,4},{14,6},{1,9},{3,11}... | collective-permute-start | bytes 1867784 | tf_op jit(solution)/shard_map/ppermute | solution.py:19
  135.3 8.5 %all-to-all-start = ((bf16[2,19,10,256]{3,1,2,0:T(8,128)(2,1)}), bf16[2,19,10,256]{3,1,2,0:T(8,128)(2,1)S(1)}, u32[]{:S(2)}, u32[]{:S(2)}) async-start(bf16[2,19,10,256]{3,1,2,0:T(8,128)(2,1)} %pad_maximum_fusion.3), calls=%async_computation | async-start | bytes 491520 | tf_op jit(solution)/shard_map/all_to_all | solution.py:131
